TPU v7x, 32 devices: a whole 2x2x4 slice. The times are simulated.
32 devices in a mesh: tm: 4 (over y, x), height: 2 (over core), chan: 4 (over z).
Axes of the slice: x: 2, y: 2, z: 4, core: 2. Of those that a mesh axis runs over, the one named last changes fastest.
Arguments:
- features: bfloat16 [384, 8, 8, 160], P('chan', 'tm', 'height'), may hold values from -400 to 400, as said below
- cotangent: bfloat16 [384, 8, 8, 160], P('chan', 'tm', 'height'), may hold values from -6 to 6
- conv_weight: bfloat16 [384, 27, 384], P('chan'), may hold values from -0.0625 to 0.0625
- norm_gain: float32 [384], replicated, may hold values from 0.5 to 1.5
- norm_bias: float32 [384], replicated, may hold values from -3 to 3
Outputs:
- input_grad: bfloat16 [384, 8, 8, 160], P('chan', 'tm', 'height')
- weight_grad: float32 [384, 27, 384], P('chan')
Inputs may be any that keep to these rules, and one draw needn't show every extreme that they name: `features`: bounded activations.
All inputs are finite; a program needn't handle non-finite values.
Results may differ from a plain program's by a relative error of at most 0.003.
Values may be sent and summed in bfloat16 or wider, within the bound.
No kernel may reach another device: no remote copies, remote signals or barrier semaphores. Data moves between devices by JAX's collectives and lax.ppermute only.
A program may use at most 64 MiB of HBM per device.

v0:
```python
import math
import jax
import jax.numpy as jnp
from jax import lax
from jax.sharding import PartitionSpec as P


def from_behind(block, axis, distance):
    devices = range(lax.axis_size(axis))
    route = [(i - distance, i) for i in devices if i - distance in devices]
    return lax.ppermute(block, axis, route)


def with_halo(array, sides, width):
    for axis, dim in sides:
        size, length = (lax.axis_size(axis), array.shape[dim])
        up = [(i, (i + 1) % size) for i in range(size - 1)]
        down = [(j, i) for i, j in up]
        last = lax.slice_in_dim(array, length - width, length, axis=dim)
        first = lax.slice_in_dim(array, 0, width, axis=dim)
        before = lax.ppermute(last, axis, up)
        after = lax.ppermute(first, axis, down)
        array = jnp.concatenate([before, array, after], axis=dim)
    return array


def on_device(features, cotangent, conv_weight, norm_gain, norm_bias):
    chans, frames, rows, cols = features.shape
    whole_x = lax.all_gather(features, "chan", axis=0, tiled=True)
    total = whole_x.shape[0]
    flat_x = whole_x.reshape(total, -1).astype(jnp.float32)
    inv_rms = lax.rsqrt(jnp.mean(flat_x * flat_x, axis=0, keepdims=True) + 1e-06)
    normed = flat_x * inv_rms * norm_gain[:, None] + norm_bias[:, None]
    active = jax.nn.silu(normed).astype(jnp.bfloat16)
    ahead = from_behind(cotangent, "tm", -1)
    longer = jnp.concatenate([cotangent, ahead], axis=1)
    bordered = with_halo(longer, (("height", 2),), 1)
    padded = jnp.pad(bordered, ((0, 0), (0, 0), (0, 0), (1, 1)))
    taps = []
    for kt in range(3):
        for kh in range(3):
            for kw in range(3):
                taps.append(
                    padded[
                        :, 2 - kt : 2 - kt + frames, 2 - kh : 2 - kh + rows, 2 - kw : 2 - kw + cols
                    ]
                )
    stacked = jnp.stack(taps, axis=1).reshape(chans * 27, -1)
    local_sums = lax.dot_general(
        stacked, active, (((1,), (1,)), ((), ())), preferred_element_type=jnp.float32
    )
    positions = frames * lax.axis_size("tm") * rows * lax.axis_size("height") * cols
    summed = lax.psum(local_sums, ("tm", "height"))
    weight_grad = (summed / math.sqrt(positions)).reshape(chans, 27, total)
    sig = jax.nn.sigmoid(normed)
    slope = sig * (1.0 + normed * (1.0 - sig))
    offset = lax.axis_index("chan") * chans
    weight_part = conv_weight.reshape(chans * 27, chans * lax.axis_size("chan"))
    act_grad = lax.psum_scatter(
        lax.dot_general(
            weight_part, stacked, (((0,), (0,)), ((), ())), preferred_element_type=jnp.float32
        ),
        "chan",
        scatter_dimension=0,
        tiled=True,
    )
    own_x = features.reshape(chans, -1).astype(jnp.float32)
    own_slope = lax.dynamic_slice_in_dim(slope, offset, chans, 0)
    own_gain = lax.dynamic_slice_in_dim(norm_gain, offset, chans, 0)
    upstream = act_grad * own_slope * own_gain[:, None]
    dots = lax.psum(jnp.sum(upstream * own_x, axis=0, keepdims=True), "chan")
    own_back = inv_rms * upstream - own_x * inv_rms**3 * dots / total
    result = cotangent.reshape(chans, -1).astype(jnp.float32) + own_back
    return (result.astype(jnp.bfloat16).reshape(features.shape), weight_grad)


def solution(mesh):
    return jax.shard_map(
        on_device,
        mesh=mesh,
        in_specs=(
            P("chan", "tm", "height", None),
            P("chan", "tm", "height", None),
            P("chan", None, None),
            P(),
            P(),
        ),
        out_specs=(P("chan", "tm", "height", None), P("chan", None, None)),
        check_vma=False,
    )
```

profile of v0, /device:TPU:0, one launch (start us, length us, event | category | flops | bytes accessed | tf_op | source)
XLA Modules:
  0.0 245.2 jit_solution(13448478375143645336)
XLA Ops:
  8.0 1.3 collective-permute-start
  9.3 1.3 copy.16
  10.7 31.4 %all_gather.3 = bf16[384,2,4,160]{3,2,1,0:T(4,128)(2,1)S(1)} all-gather(bf16[96,2,4,160]{3,2,1,0:T(4,128)(2,1)S(1)} %copy.16), channel_id=1, replica_groups=mesh['tm'=4,'height'=2,'chan'=4] {'chan'}, dimensions={0}, use_global_device_ids=true | all-gather | bytes 1228800 | tf_op jit(solution)/shard_map/all_gather | solution.py:29
  42.1 1.4 copy.17
  43.9 1.0 constant_dynamic-update-slice_fusion.1
  45.0 1.3 collective-permute-start.1
  46.3 1.3 collective-permute-start.2
  47.6 1.4 multiply_convert_fusion
  71.3 21.1 %copy.18 = bf16[96,27,2,4,160]{4,3,2,1,0:T(4,128)(2,1)} copy(bf16[96,27,2,4,160]{0,4,3,2,1:T(8,128)(2,1)} %fusion.31) | data formatting | bytes 13271040 | tf_op jit(solution)/shard_map/stack | solution.py:48
  92.5 20.4 %reshape.67 = bf16[2592,1280]{1,0:T(8,128)(2,1)} reshape(bf16[96,27,2,4,160]{4,3,2,1,0:T(4,128)(2,1)} %copy.18) | data formatting | bytes 13271040 | tf_op jit(solution)/shard_map/reshape | solution.py:48
  112.8 8.4 %fusion.56 = f32[2592,384]{1,0:T(8,128)} fusion(bf16[2592,1280]{1,0:T(8,128)(2,1)} %reshape.67, bf16[384,1280]{0,1:T(8,128)(2,1)S(1)} %bitcast.128), kind=kOutput, calls=%fused_computation.102 | convolution fusion | flops 2548039680 | bytes 11599872 | tf_op jit(solution)/shard_map/dot_general | solution.py:49
  121.5 2.3 copy.19
  123.8 2.2 reshape.68
  126.0 6.7 %convolution_bitcast_fusion = f32[384,1280]{0,1:T(8,128)S(1)} fusion(bf16[2592,1280]{1,0:T(8,128)(2,1)} %reshape.67, bf16[2592,384]{1,0:T(8,128)(2,1)} %reshape.68), kind=kOutput, calls=%fused_computation.2 | convolution fusion | flops 2548039680 | bytes 10592256 | tf_op jit(solution)/shard_map/dot_general | solution.py:60
  132.7 1.8 copy.21
  134.7 1.8 negate_exponential_fusion
  136.5 66.4 %all-reduce.3.cloned.1.call-done = f32[2592,384]{1,0:T(8,128)} async-done(((f32[2592,384]{1,0:T(8,128)}), f32[2592,384]{1,0:T(8,128)}) %all-reduce.3.cloned.1.call-update) | async-done | bytes 3981328 | tf_op jit(solution)/shard_map/psum | solution.py:53
  202.9 4.4 %broadcast_multiply_fusion = f32[2592,384]{1,0:T(8,128)} fusion(f32[2592,384]{1,0:T(8,128)} %all-reduce.3.cloned.1.call-done), kind=kLoop, calls=%fused_computation.4 | loop fusion | flops 995328 | bytes 7962624 | tf_op jit(solution)/shard_map/div | solution.py:54
  207.3 5.0 %reshape.70 = f32[96,27,384]{2,1,0:T(8,128)} reshape(f32[2592,384]{1,0:T(8,128)} %broadcast_multiply_fusion) | data formatting | bytes 7962624 | tf_op jit(solution)/shard_map/reshape | solution.py:54
  212.3 6.6 %copy.20 = f32[96,27,384]{2,0,1:T(8,128)} copy(f32[96,27,384]{2,1,0:T(8,128)} %reshape.70) | data formatting | bytes 7962624
  218.8 2.1 copy.22
  221.0 2.8 %fusion.13 = (f32[1280]{0:T(1024)S(1)}, f32[96,1280]{0,1:T(8,128)}) fusion(bf16[96,2,4,160]{0,3,2,1:T(8,128)(2,1)S(1)} %copy-done.2, f32[96]{0:T(128)S(1)} %dynamic_slice.7, f32[96,1280]{0,1:T(8,128)} %copy.22, f32[384,1280]{0,1:T(8,128)} %get-tuple-element.13, s32[]{:T(128)S(6)} %select_n.4, f32[384,1280]{0,1:T(8,128)S(1)} %get-tuple-element.12), kind=kLoop, calls=%fused_computation.31 | loop fusion | flops 1350400 | bytes 2217348 | tf_op jit(solution)/shard_map/reduce_sum | solution.py:71
  223.8 11.6 %psum.14 = f32[1280]{0:T(1024)S(1)} all-reduce(f32[1280]{0:T(1024)S(1)} %get-tuple-element.10), channel_id=1, replica_groups=mesh['tm'=4,'height'=2,'chan'=4] {'chan'}, use_global_device_ids=true, to_apply=%region_3.4 | all-reduce | flops 1280 | bytes 10240 | tf_op jit(solution)/shard_map/psum | solution.py:71
  235.4 2.4 fusion.12
  (53 shorter events, 23.2 us)
Async XLA Ops:
  8.0 194.9 %all-reduce.3.cloned.1.call-start = ((), (), s32[]{:S(2)}) async-start(), calls=%async_computation.1 | async-start | bytes 7962624 | tf_op jit(solution)/shard_map/psum | solution.py:53
  8.0 36.9 %collective-permute-start = (bf16[96,2,4,160]{0,3,2,1:T(8,128)(2,1)}, bf16[96,2,4,160]{0,3,2,1:T(8,128)(2,1)S(1)}, u32[]{:S(2)}, u32[]{:S(2)}) collective-permute-start(bf16[96,2,4,160]{0,3,2,1:T(8,128)(2,1)} %param.6), channel_id=1, source_target_pairs={{8,0},{16,8},{24,16},{9,1},{17,9},{25,17},{10,2},{18,10},{26,18},{... | collective-permute-start | bytes 737288 | tf_op jit(solution)/shard_map/ppermute | solution.py:11
  45.0 4.0 %collective-permute-start.1 = (bf16[96,4,1,160]{0,3,2,1:T(8,128)(2,1)S(1)}, bf16[96,4,1,160]{0,3,2,1:T(8,128)(2,1)S(1)}, u32[]{:S(2)}, u32[]{:S(2)}) collective-permute-start(bf16[96,4,1,160]{0,3,2,1:T(8,128)(2,1)S(1)} %get-tuple-element.14), channel_id=1, source_target_pairs={{0,4},{1,5},{2,6},{3,7},{8,12},{9,13},{10,14},{11,15},{16,20},{17,... | collective-permute-start | bytes 368648 | tf_op jit(solution)/shard_map/ppermute | solution.py:21
  46.3 3.3 %collective-permute-start.2 = (bf16[96,4,1,160]{0,3,2,1:T(8,128)(2,1)S(1)}, bf16[96,4,1,160]{0,3,2,1:T(8,128)(2,1)S(1)}, u32[]{:S(2)}, u32[]{:S(2)}) collective-permute-start(bf16[96,4,1,160]{0,3,2,1:T(8,128)(2,1)S(1)} %get-tuple-element.15), channel_id=1, source_target_pairs={{4,0},{5,1},{6,2},{7,3},{12,8},{13,9},{14,10},{15,11},{20,16},{21,... | collective-permute-start | bytes 368648 | tf_op jit(solution)/shard_map/ppermute | solution.py:22
  50.0 17.4 %copy-start = (bf16[96,2,4,160]{0,3,2,1:T(8,128)(2,1)S(1)}, bf16[96,2,4,160]{0,3,2,1:T(8,128)(2,1)}, u32[]{:S(2)}) copy-start(bf16[96,2,4,160]{0,3,2,1:T(8,128)(2,1)} %param.6) | copy-start | bytes 737284
  121.3 97.5 %reduce-scatter.4.cloned.1.call-start = ((), (), s32[]{:S(2)}) async-start(), calls=%async_computation.2 | async-start | bytes 2457600
  126.0 8.6 %copy-start.3 = (f32[384]{0:T(512)S(1)}, f32[384]{0:T(512)}, u32[]{:S(2)}) copy-start(f32[384]{0:T(512)} %param.8) | copy-start | bytes 4612
  126.0 8.7 %copy-start.4 = (f32[384]{0:T(512)S(1)}, f32[384]{0:T(512)}, u32[]{:S(2)}) copy-start(f32[384]{0:T(512)} %param.9) | copy-start | bytes 4612
  207.3 13.7 %copy-start.2 = (bf16[96,2,4,160]{0,3,2,1:T(8,128)(2,1)S(1)}, bf16[96,2,4,160]{0,3,2,1:T(8,128)(2,1)}, u32[]{:S(2)}) copy-start(bf16[96,2,4,160]{0,3,2,1:T(8,128)(2,1)} %param.5) | copy-start | bytes 737284
  207.3 28.1 %copy-start.1 = (bf16[96,2,4,160]{0,3,2,1:T(8,128)(2,1)S(1)}, bf16[96,2,4,160]{0,3,2,1:T(8,128)(2,1)}, u32[]{:S(2)}) copy-start(bf16[96,2,4,160]{0,3,2,1:T(8,128)(2,1)} %param.6) | copy-start | bytes 737284
Sparse Core Ops, SparseCore 0:
  121.4 81.3 all-reduce.2
Sparse Core Ops, SparseCore 1:
  134.6 44.6 reduce-scatter.3
where the time goes:
time: 247 us; the launch traced here: 245 us
  local copies, waits for them, and re-layouts  82 us (33%)
  waiting for transfers between devices  67 us (27%)
  blocking collectives  43 us (17%)
  other arithmetic  18.3 us (7%)
  between operations  15.6 us (6%)
  matrix products  15.1 us (6%)
  starting transfers between devices  4.15 us (2%)
    psum x1, waiting for transfers between devices, on_device(): summed = lax.psum(local_sums, ('tm', 'height'))  66.4 us
    all_gather x1, blocking collectives, on_device(): whole_x = lax.all_gather(features, 'chan', axis=0, tiled=True)  31.4 us
    unnamed x36, local copies, waits for them, and re-layouts  30.9 us
    another operation x2, local copies, waits for them, and re-layouts, on_device(): stacked = jnp.stack(taps, axis=1).reshape(chans * 27, -1)  21.9 us
    reshape x1, local copies, waits for them, and re-layouts, on_device(): stacked = jnp.stack(taps, axis=1).reshape(chans * 27, -1)  20.4 us
    psum x1, blocking collectives, on_device(): dots = lax.psum(jnp.sum(upstream * own_x, axis=0, keepdims=True), 'chan')  11.6 us
    dot_general x1, matrix products, on_device(): lax.dot_general(stacked, active, (((1,), (1,)), ((), ())), preferred_elem...  8.42 us
    dot_general x1, matrix products, on_device(): lax.dot_general(weight_part, stacked, (((0,), (0,)), ((), ())), preferred...  6.67 us
  transfers between devices with their start and end apart: 5, of which 2 were waited for; matrix products, arithmetic and copies ran while one was open for 15% of the time, Pallas kernels for 0%

commit v1 on v0

--- a/solution.py
+++ b/solution.py
@@ -1,8 +1,36 @@
+import functools
 import math
 import jax
 import jax.numpy as jnp
 from jax import lax
 from jax.sharding import PartitionSpec as P
+
+
+def move_grid_on(vector, axis_id):
+    big, current_block, lower = (lax.axis_size(axis_id), lax.axis_index(axis_id), vector.shape[0])
+    xs_all = [to_i * big if num == 0 else to_i for num, to_i in enumerate(vector.shape)]
+    o_now = current_arr = vector
+    v1 = lax.dynamic_update_slice_in_dim(
+        jnp.zeros(xs_all, vector.dtype), vector, current_block * lower, axis=0
+    )
+    for p in range(1, big // 2 + 1):
+        o_now = lax.ppermute(
+            o_now, axis_id, perm=list(map(lambda num: (num, (num + 1) % big), range(big)))
+        )
+        v1 = lax.dynamic_update_slice_in_dim(v1, o_now, (current_block - p) % big * lower, axis=0)
+        if 2 * p < big:
+            current_arr = lax.ppermute(
+                current_arr,
+                axis_name=axis_id,
+                perm=list(map(lambda num: (num, (num - 1) % big), range(big))),
+            )
+            v1 = lax.dynamic_update_slice_in_dim(
+                v1, current_arr, (current_block + p) % big * lower, axis=0
+            )
+    return v1
+
+
+scan_stops_all = functools.partial(move_grid_on, axis_id="chan")
 
 
 def from_behind(block, axis, distance):
@@ -26,7 +54,7 @@
 
 def on_device(features, cotangent, conv_weight, norm_gain, norm_bias):
     chans, frames, rows, cols = features.shape
-    whole_x = lax.all_gather(features, "chan", axis=0, tiled=True)
+    whole_x = scan_stops_all(features)
     total = whole_x.shape[0]
     flat_x = whole_x.reshape(total, -1).astype(jnp.float32)
     inv_rms = lax.rsqrt(jnp.mean(flat_x * flat_x, axis=0, keepdims=True) + 1e-06)

time: 247 us -> 231 us (0.935)
  blocking collectives: 43 us -> 11.4 us
  local copies, waits for them, and re-layouts: 82 us -> 95.5 us
  starting transfers between devices: 4.15 us -> 12.5 us
  waiting for transfers between devices: 67 us -> 60.6 us
    all_gather x1 -> x0, blocking collectives: 31.4 us -> none  [on_device(): whole_x = lax.all_gather(features, 'chan', axis=0, tiled=True)]
    dynamic_update_slice x0 -> x4, local copies, waits for them, and re-layouts: none -> 11.9 us  [the longest x2 5.98 us: move_grid_on(): lax.dynamic_update_slice_in_dim(v1, o_now, (current_block - p) % big * lo...]
    psum x1, waiting for transfers between devices: 66.4 us -> 55.3 us  [on_device(): summed = lax.psum(local_sums, ('tm', 'height'))]
    ppermute x0 -> x3, starting transfers between devices: none -> 8.33 us  [the longest x2 6.24 us: move_grid_on(): lax.ppermute(o_now, axis_id, perm=list(map(lambda num: (num, (num + 1) %...]
    ppermute x1, waiting for transfers between devices: 0.01 us -> 5.29 us  [from_behind(): return lax.ppermute(block, axis, route)]
    unnamed x36 -> x33, local copies, waits for them, and re-layouts: 30.9 us -> 31.1 us
  transfers between devices with their start and end apart: 5 -> 8, of which waited for: 2 -> 2; matrix products, arithmetic and copies ran while one was open for 15% -> 49% of each run, Pallas kernels for 0% -> 0%
where the time goes in v1:
time: 231 us; the launch traced here: 230 us
  local copies, waits for them, and re-layouts  95.5 us (41%)
  waiting for transfers between devices  60.6 us (26%)
  matrix products  17.3 us (7%)
  other arithmetic  16.7 us (7%)
  between operations  15.7 us (7%)
  starting transfers between devices  12.5 us (5%)
  blocking collectives  11.4 us (5%)
    psum x1, waiting for transfers between devices, on_device(): summed = lax.psum(local_sums, ('tm', 'height'))  55.3 us
    unnamed x33, local copies, waits for them, and re-layouts  31.1 us
    another operation x2, local copies, waits for them, and re-layouts, on_device(): stacked = jnp.stack(taps, axis=1).reshape(chans * 27, -1)  21.8 us
    reshape x1, local copies, waits for them, and re-layouts, on_device(): stacked = jnp.stack(taps, axis=1).reshape(chans * 27, -1)  20.4 us
    psum x1, blocking collectives, on_device(): dots = lax.psum(jnp.sum(upstream * own_x, axis=0, keepdims=True), 'chan')  11.4 us
    dot_general x1, matrix products, on_device(): lax.dot_general(weight_part, stacked, (((0,), (0,)), ((), ())), preferred...  8.82 us
    dot_general x1, matrix products, on_device(): lax.dot_general(stacked, active, (((1,), (1,)), ((), ())), preferred_elem...  8.44 us
    ppermute x2, starting transfers between devices, move_grid_on(): lax.ppermute(o_now, axis_id, perm=list(map(lambda num: (num, (num + 1) %...  6.24 us
  transfers between devices with their start and end apart: 8, of which 2 were waited for; matrix products, arithmetic and copies ran while one was open for 49% of the time, Pallas kernels for 0%

profile of v1, /device:TPU:0, one launch (start us, length us, event | category | flops | bytes accessed | tf_op | source)
XLA Modules:
  0.0 229.7 jit_solution(13244334050588449443)
XLA Ops:
  8.0 1.3 collective-permute-start.3
  9.3 3.1 %collective-permute-start = (bf16[96,2,4,160]{0,3,2,1:T(8,128)(2,1)}, bf16[96,2,4,160]{0,3,2,1:T(8,128)(2,1)S(1)}, u32[]{:S(2)}, u32[]{:S(2)}) collective-permute-start(bf16[96,2,4,160]{0,3,2,1:T(8,128)(2,1)} %param.5), channel_id=1, source_target_pairs={{0,1},{1,2},{2,3},{3,0},{4,5},{5,6},{6,7},{7,4},{8,9},{9,10},{10,1... | collective-permute-start | bytes 737288 | tf_op jit(solution)/shard_map/ppermute | solution.py:17
  12.4 2.1 collective-permute-start.1
  15.5 5.3 %collective-permute-done.3 = bf16[96,2,4,160]{0,3,2,1:T(8,128)(2,1)S(1)} collective-permute-done((bf16[96,2,4,160]{0,3,2,1:T(8,128)(2,1)}, bf16[96,2,4,160]{0,3,2,1:T(8,128)(2,1)S(1)}, u32[]{:S(2)}, u32[]{:S(2)}) %collective-permute-start.3) | collective-permute-done | bytes 245792 | tf_op jit(solution)/shard_map/ppermute | solution.py:39
  24.3 2.8 %dynamic_update_slice.12 = bf16[384,2,4,160]{0,3,2,1:T(8,128)(2,1)S(1)} dynamic-update-slice(bf16[384,2,4,160]{0,3,2,1:T(8,128)(2,1)S(1)} %broadcast_in_dim.4, bf16[96,2,4,160]{0,3,2,1:T(8,128)(2,1)} %param.5, s32[]{:T(128)S(6)} %select_n.29, s32[]{:T(128)} %constant.44.clone.1, s32[]{:T(128)} %constant.44.clone.1, s32[]{:T(128)} %constant.44.clone.1) | dynamic-update-slice | bytes 491524 | tf_op jit(solution)/shard_map/dynamic_update_slice | solution.py:13
  27.1 3.2 %collective-permute-start.2 = (bf16[96,2,4,160]{0,3,2,1:T(8,128)(2,1)S(1)}, bf16[96,2,4,160]{0,3,2,1:T(8,128)(2,1)S(1)}, u32[]{:S(2)}, u32[]{:S(2)}) collective-permute-start(bf16[96,2,4,160]{0,3,2,1:T(8,128)(2,1)S(1)} %collective-permute-done), channel_id=1, source_target_pairs={{0,1},{1,2},{2,3},{3,0},{4,5},{5,6},{6,7},{7,4},{8,9},{9,10},{10,1... | collective-permute-start | bytes 737288 | tf_op jit(solution)/shard_map/ppermute | solution.py:17
  30.2 2.9 %dynamic_update_slice.13 = bf16[384,2,4,160]{0,3,2,1:T(8,128)(2,1)S(1)} dynamic-update-slice(bf16[384,2,4,160]{0,3,2,1:T(8,128)(2,1)S(1)} %dynamic_update_slice.12, bf16[96,2,4,160]{0,3,2,1:T(8,128)(2,1)S(1)} %collective-permute-done, s32[]{:T(128)S(6)} %select_n.31, s32[]{:T(128)} %constant.44.clone.1, s32[]{:T(128)} %constant.44.clone.1, s32[]{:T(128)} %constant.44.clone.1) | dynamic-update-slice | bytes 491524 | tf_op jit(solution)/shard_map/dynamic_update_slice | solution.py:20
  33.1 3.1 %dynamic_update_slice.14 = bf16[384,2,4,160]{0,3,2,1:T(8,128)(2,1)S(1)} dynamic-update-slice(bf16[384,2,4,160]{0,3,2,1:T(8,128)(2,1)S(1)} %dynamic_update_slice.13, bf16[96,2,4,160]{0,3,2,1:T(8,128)(2,1)S(1)} %collective-permute-done.1, s32[]{:T(128)S(6)} %select_n.33, s32[]{:T(128)} %constant.44.clone.1, s32[]{:T(128)} %constant.44.clone.1, s32[]{:T(128)} %constant.44.clone.1) | dynamic-update-slice | bytes 491524 | tf_op jit(solution)/shard_map/dynamic_update_slice | solution.py:27
  57.9 21.1 %copy.11 = bf16[96,27,2,4,160]{4,3,2,1,0:T(4,128)(2,1)} copy(bf16[96,27,2,4,160]{0,4,3,2,1:T(8,128)(2,1)} %fusion.31) | data formatting | bytes 13271040 | tf_op jit(solution)/shard_map/stack | solution.py:76
  78.9 20.4 %reshape.67 = bf16[2592,1280]{1,0:T(8,128)(2,1)} reshape(bf16[96,27,2,4,160]{4,3,2,1,0:T(4,128)(2,1)} %copy.11) | data formatting | bytes 13271040 | tf_op jit(solution)/shard_map/reshape | solution.py:76
  99.4 3.1 %dynamic_update_slice.15 = bf16[384,2,4,160]{0,3,2,1:T(8,128)(2,1)S(1)} dynamic-update-slice(bf16[384,2,4,160]{0,3,2,1:T(8,128)(2,1)S(1)} %dynamic_update_slice.14, bf16[96,2,4,160]{0,3,2,1:T(8,128)(2,1)S(1)} %collective-permute-done.2, s32[]{:T(128)S(6)} %select_n.35, s32[]{:T(128)} %constant.44.clone.1, s32[]{:T(128)} %constant.44.clone.1, s32[]{:T(128)} %constant.44.clone.1) | dynamic-update-slice | bytes 491524 | tf_op jit(solution)/shard_map/dynamic_update_slice | solution.py:20
  103.6 8.4 %fusion.56 = f32[2592,384]{1,0:T(8,128)} fusion(bf16[2592,1280]{1,0:T(8,128)(2,1)} %reshape.67, bf16[384,1280]{0,1:T(8,128)(2,1)S(1)} %bitcast.128), kind=kOutput, calls=%fused_computation.102 | convolution fusion | flops 2548039680 | bytes 11599872 | tf_op jit(solution)/shard_map/dot_general | solution.py:77
  112.3 3.7 %copy.12 = bf16[96,27,384]{2,1,0:T(8,128)(2,1)} copy(bf16[96,27,384]{2,0,1:T(8,128)(2,1)} %param.7) | data formatting | bytes 3981312 | tf_op args[2]
  116.0 4.3 %reshape.68 = bf16[2592,384]{1,0:T(8,128)(2,1)} reshape(bf16[96,27,384]{2,1,0:T(8,128)(2,1)} %copy.12) | data formatting | bytes 3981312 | tf_op jit(solution)/shard_map/reshape | solution.py:86
  120.3 8.8 %convolution_bitcast_fusion = f32[384,1280]{0,1:T(8,128)} fusion(bf16[2592,1280]{1,0:T(8,128)(2,1)} %reshape.67, bf16[2592,384]{1,0:T(8,128)(2,1)} %reshape.68), kind=kOutput, calls=%fused_computation.2 | convolution fusion | flops 2548039680 | bytes 10592256 | tf_op jit(solution)/shard_map/dot_general | solution.py:88
  129.1 2.9 %copy.14 = f32[384,1280]{1,0:T(8,128)} copy(f32[384,1280]{0,1:T(8,128)} %convolution_bitcast_fusion) | data formatting | bytes 3932160
  132.2 2.4 %negate_exponential_fusion = (f32[384,1280]{0,1:T(8,128)}, f32[384,1280]{0,1:T(8,128)}) fusion(f32[384]{0:T(512)S(1)} %copy-done.3, f32[384]{0:T(512)S(1)} %copy-done.2, f32[1280]{0:T(1024)S(1)} %rsqrt.16, bf16[384,2,4,160]{0,3,2,1:T(8,128)(2,1)S(1)} %dynamic_update_slice.15), kind=kLoop, calls=%fused_computation.9 | loop fusion | flops 2457600 | bytes 4923392 | tf_op jit(solution)/shard_map/exp | solution.py:83
  134.7 55.3 %all-reduce.3.cloned.1.call-done = f32[2592,384]{1,0:T(8,128)} async-done(((f32[2592,384]{1,0:T(8,128)}), f32[2592,384]{1,0:T(8,128)}) %all-reduce.3.cloned.1.call-update) | async-done | bytes 3981328 | tf_op jit(solution)/shard_map/psum | solution.py:81
  189.9 4.4 %broadcast_multiply_fusion = f32[2592,384]{1,0:T(8,128)} fusion(f32[2592,384]{1,0:T(8,128)} %all-reduce.3.cloned.1.call-done), kind=kLoop, calls=%fused_computation.4 | loop fusion | flops 995328 | bytes 7962624 | tf_op jit(solution)/shard_map/div | solution.py:82
  194.3 5.0 %reshape.70 = f32[96,27,384]{2,1,0:T(8,128)} reshape(f32[2592,384]{1,0:T(8,128)} %broadcast_multiply_fusion) | data formatting | bytes 7962624 | tf_op jit(solution)/shard_map/reshape | solution.py:82
  199.3 6.6 %copy.13 = f32[96,27,384]{2,0,1:T(8,128)} copy(f32[96,27,384]{2,1,0:T(8,128)} %reshape.70) | data formatting | bytes 7962624
  207.2 2.3 %fusion.13 = (f32[1280]{0:T(1024)S(1)}, f32[96,1280]{0,1:T(8,128)S(1)}) fusion(bf16[96,2,4,160]{0,3,2,1:T(8,128)(2,1)S(1)} %copy-done.1, f32[96]{0:T(128)S(1)} %dynamic_slice.7, f32[96,1280]{0,1:T(8,128)S(1)} %copy.15, f32[384,1280]{0,1:T(8,128)} %get-tuple-element.11, s32[]{:T(128)S(6)} %select_n.29, f32[384,1280]{0,1:T(8,128)} %get-tuple-element.10), kind=kLoop, calls=%fused_computation.31 | loop fusion | flops 1350400 | bytes 2217348 | tf_op jit(solution)/shard_map/reduce_sum | solution.py:99
  209.5 11.4 %psum.14 = f32[1280]{0:T(1024)S(1)} all-reduce(f32[1280]{0:T(1024)S(1)} %get-tuple-element.8), channel_id=1, replica_groups=mesh['tm'=4,'height'=2,'chan'=4] {'chan'}, use_global_device_ids=true, to_apply=%region_3.4 | all-reduce | flops 1280 | bytes 10240 | tf_op jit(solution)/shard_map/psum | solution.py:99
  220.9 1.3 fusion.12
  (59 shorter events, 28.7 us)
Async XLA Ops:
  8.0 181.9 %all-reduce.3.cloned.1.call-start = ((), (), s32[]{:S(2)}) async-start(), calls=%async_computation.1 | async-start | bytes 7962624 | tf_op jit(solution)/shard_map/psum | solution.py:81
  8.0 12.8 %collective-permute-start.3 = (bf16[96,2,4,160]{0,3,2,1:T(8,128)(2,1)}, bf16[96,2,4,160]{0,3,2,1:T(8,128)(2,1)S(1)}, u32[]{:S(2)}, u32[]{:S(2)}) collective-permute-start(bf16[96,2,4,160]{0,3,2,1:T(8,128)(2,1)} %param.6), channel_id=1, source_target_pairs={{8,0},{16,8},{24,16},{9,1},{17,9},{25,17},{10,2},{18,10},{26,18},{... | collective-permute-start | bytes 737288 | tf_op jit(solution)/shard_map/ppermute | solution.py:39
  9.3 17.7 %collective-permute-start = (bf16[96,2,4,160]{0,3,2,1:T(8,128)(2,1)}, bf16[96,2,4,160]{0,3,2,1:T(8,128)(2,1)S(1)}, u32[]{:S(2)}, u32[]{:S(2)}) collective-permute-start(bf16[96,2,4,160]{0,3,2,1:T(8,128)(2,1)} %param.5), channel_id=1, source_target_pairs={{0,1},{1,2},{2,3},{3,0},{4,5},{5,6},{6,7},{7,4},{8,9},{9,10},{10,1... | collective-permute-start | bytes 737288 | tf_op jit(solution)/shard_map/ppermute | solution.py:17
  12.4 20.7 %collective-permute-start.1 = (bf16[96,2,4,160]{0,3,2,1:T(8,128)(2,1)}, bf16[96,2,4,160]{0,3,2,1:T(8,128)(2,1)S(1)}, u32[]{:S(2)}, u32[]{:S(2)}) collective-permute-start(bf16[96,2,4,160]{0,3,2,1:T(8,128)(2,1)} %param.5), channel_id=1, source_target_pairs={{0,3},{1,0},{2,1},{3,2},{4,7},{5,4},{6,5},{7,6},{8,11},{9,8},{10,9... | collective-permute-start | bytes 737288 | tf_op jit(solution)/shard_map/ppermute | solution.py:22
  21.5 14.7 %collective-permute-start.4 = (bf16[96,4,1,160]{0,3,2,1:T(8,128)(2,1)}, bf16[96,4,1,160]{0,3,2,1:T(8,128)(2,1)S(1)}, u32[]{:S(2)}, u32[]{:S(2)}) collective-permute-start(bf16[96,4,1,160]{0,3,2,1:T(8,128)(2,1)} %get-tuple-element.12), channel_id=1, source_target_pairs={{0,4},{1,5},{2,6},{3,7},{8,12},{9,13},{10,14},{11,15},{16,20},{17,... | collective-permute-start | bytes 368648 | tf_op jit(solution)/shard_map/ppermute | solution.py:49
  22.8 13.5 %collective-permute-start.5 = (bf16[96,4,1,160]{0,3,2,1:T(8,128)(2,1)S(1)}, bf16[96,4,1,160]{0,3,2,1:T(8,128)(2,1)S(1)}, u32[]{:S(2)}, u32[]{:S(2)}) collective-permute-start(bf16[96,4,1,160]{0,3,2,1:T(8,128)(2,1)S(1)} %get-tuple-element.13), channel_id=1, source_target_pairs={{4,0},{5,1},{6,2},{7,3},{12,8},{13,9},{14,10},{15,11},{20,16},{21,... | collective-permute-start | bytes 368648 | tf_op jit(solution)/shard_map/ppermute | solution.py:50
  27.1 72.3 %collective-permute-start.2 = (bf16[96,2,4,160]{0,3,2,1:T(8,128)(2,1)S(1)}, bf16[96,2,4,160]{0,3,2,1:T(8,128)(2,1)S(1)}, u32[]{:S(2)}, u32[]{:S(2)}) collective-permute-start(bf16[96,2,4,160]{0,3,2,1:T(8,128)(2,1)S(1)} %collective-permute-done), channel_id=1, source_target_pairs={{0,1},{1,2},{2,3},{3,0},{4,5},{5,6},{6,7},{7,4},{8,9},{9,10},{10,1... | collective-permute-start | bytes 737288 | tf_op jit(solution)/shard_map/ppermute | solution.py:17
  36.7 17.3 %copy-start = (bf16[96,2,4,160]{0,3,2,1:T(8,128)(2,1)S(1)}, bf16[96,2,4,160]{0,3,2,1:T(8,128)(2,1)}, u32[]{:S(2)}) copy-start(bf16[96,2,4,160]{0,3,2,1:T(8,128)(2,1)} %param.6) | copy-start | bytes 737284
  78.9 23.9 %copy-start.2 = (f32[384]{0:T(512)S(1)}, f32[384]{0:T(512)}, u32[]{:S(2)}) copy-start(f32[384]{0:T(512)} %param.8) | copy-start | bytes 4612
  78.9 23.9 %copy-start.3 = (f32[384]{0:T(512)S(1)}, f32[384]{0:T(512)}, u32[]{:S(2)}) copy-start(f32[384]{0:T(512)} %param.9) | copy-start | bytes 4612
  112.0 93.8 %reduce-scatter.4.cloned.1.call-start = ((), (), s32[]{:S(2)}) async-start(), calls=%async_computation.2 | async-start | bytes 2457600
  194.3 12.8 %copy-start.1 = (bf16[96,2,4,160]{0,3,2,1:T(8,128)(2,1)S(1)}, bf16[96,2,4,160]{0,3,2,1:T(8,128)(2,1)}, u32[]{:S(2)}) copy-start(bf16[96,2,4,160]{0,3,2,1:T(8,128)(2,1)} %param.5) | copy-start | bytes 737284
Sparse Core Ops, SparseCore 0:
  112.2 77.7 all-reduce.2
Sparse Core Ops, SparseCore 1:
  132.2 40.2 reduce-scatter.3
